TPU v7x, 32 devices: a whole 2x2x4 slice. The times are simulated.
32 devices in a mesh: groups: 2 (over x), wide: 4 (over y, core), expert: 4 (over z).
Axes of the slice: x: 2, y: 2, z: 4, core: 2. Of those that a mesh axis runs over, the one named last changes fastest.
Arguments:
- prompts: bfloat16 [8, 128, 6144], P(('groups', 'wide'), None, 'expert'), parts along dimension 0, may hold values from -6 to 6
- span_slot_owner: int32 [8], P('groups'), parts along dimension 0, may hold values from 0 to 3, as said below
- row_expert_index: int32 [768, 2], P('groups'), parts along dimension 0, may hold values from 0 to 7, all different within a row
- tile_tenant_index: int32 [6], P('groups'), parts along dimension 0, may hold values from 0 to 7
- tenant_adapter_slot: int32 [16], P('groups'), parts along dimension 0, may hold values from 0 to 7, each once
- router: bfloat16 [6144, 8], replicated, may hold values from -0.078125 to 0.078125
- gate_weight: bfloat16 [2, 6144, 16384], P(None, None, ('wide', 'expert')), may hold values from -0.078125 to 0.078125
- up_weight: bfloat16 [2, 6144, 16384], P(None, None, ('wide', 'expert')), may hold values from -0.078125 to 0.078125
- down_weight: bfloat16 [2, 16384, 6144], P(None, 'wide', 'expert'), may hold values from -0.046875 to 0.046875
- adapter_down_weight: bfloat16 [16, 2, 6144, 64], P(('groups', 'wide'), None, 'expert'), parts along dimension 0, may hold values from -0.078125 to 0.078125
- adapter_up_weight: bfloat16 [16, 2, 64, 16384], P('groups', None, None, ('wide', 'expert')), parts along dimension 0, may hold values from -0.75 to 0.75
Outputs:
- mixed: bfloat16 [768, 6144], P(('groups', 'wide'), 'expert'), parts along dimension 0
There are 2 independent parts, one for each index of `groups`. A program takes and returns all parts, laid end to end along the dimension named above; an argument that names none is the same for every part. Nothing has to cross between parts.
Inputs may be any that keep to these rules, and one draw needn't show every extreme that they name: `span_slot_owner`: a permutation of the slots; span c, for c < 3, is in slot span_slot_owner[c]. `row_expert_index`: each row names two different experts. `tenant_adapter_slot`: a permutation of the slots. `tile_tenant_index`: tenant of rows 128 * i to 128 * i + 127.
All inputs are finite; a program needn't handle non-finite values.
Results may differ from a plain program's by a relative error of at most 0.0051.
Values may be sent and summed in bfloat16 or wider, within the bound.
No kernel may reach another device: no remote copies, remote signals or barrier semaphores. Data moves between devices by JAX's collectives and lax.ppermute only.
A program may use at most 128 MiB of HBM per device.

v0:
```python
import jax
import jax.numpy as jnp
import numpy as np
from jax import lax
from jax.sharding import Mesh
from jax.sharding import PartitionSpec as P

ADAPTER_SCALE = 0.5
WIDE = ("wy", "wc")
GROUP = ("wy", "wc", "expert")


def per_device(
    prompts,
    span_slot_owner,
    row_expert_index,
    tile_tenant_index,
    tenant_adapter_slot,
    router,
    gate_weight,
    up_weight,
    down_weight,
    adapter_down_weight,
    adapter_up_weight,
):
    span = prompts.shape[1]
    quarter = prompts.shape[2]
    tokens = row_expert_index.shape[0]
    nchunk = tokens // span
    window = gate_weight.shape[0]
    core = lax.axis_index("wc")
    cores = lax.axis_size("wc")
    wide_index = lax.axis_index(WIDE)
    slots_q = lax.all_gather(prompts, WIDE, axis=0, tiled=True)
    rows_q = jnp.take(slots_q, span_slot_owner[:nchunk], axis=0).reshape(tokens, quarter)
    half = tokens // cores
    mine_q = lax.dynamic_slice_in_dim(rows_q, core * half, half, 0)
    mine = lax.all_gather(mine_q, "expert", axis=1, tiled=True)
    other = lax.ppermute(mine, "wc", [(i, (i + 1) % cores) for i in range(cores)])
    first = jnp.where(core == 0, mine, other)
    second = jnp.where(core == 0, other, mine)
    input_rows = jnp.concatenate([first, second], axis=0)
    logits = jnp.dot(input_rows, router, preferred_element_type=jnp.float32)
    experts = jnp.arange(router.shape[1], dtype=jnp.int32)
    picked = (row_expert_index[:, :, None] == experts[None, None, :]).astype(jnp.float32)
    chosen = jnp.sum(picked * logits[:, None, :], axis=2)
    first_prob = jax.nn.sigmoid(chosen[:, 0] - chosen[:, 1])
    second_prob = jax.nn.sigmoid(chosen[:, 1] - chosen[:, 0])
    weight = (
        first_prob[:, None] * picked[:, 0, :window] + second_prob[:, None] * picked[:, 1, :window]
    )
    tile_count = tile_tenant_index.shape[0]
    tile_rows = tokens // tile_count
    resident_slots = adapter_down_weight.shape[0]
    tile_slot_index = jnp.take(tenant_adapter_slot, tile_tenant_index)
    owners = tile_slot_index // resident_slots
    local_index = tile_slot_index % resident_slots
    held = jnp.take(adapter_down_weight, local_index, axis=0)
    partial_rank = jnp.einsum(
        "ntd,nedr->nter",
        rows_q.reshape(tile_count, tile_rows, quarter),
        held,
        preferred_element_type=jnp.float32,
    )
    partial_rank = jnp.where(
        (owners == wide_index)[:, None, None, None], partial_rank, jnp.zeros_like(partial_rank)
    )
    lowrank = lax.reduce_precision(lax.psum(partial_rank, GROUP), exponent_bits=8, mantissa_bits=7)
    tile_up = jnp.take(adapter_up_weight, tile_tenant_index, axis=0)
    adapted_hidden = jnp.einsum(
        "nter,nerf->ntef", lowrank, tile_up.astype(jnp.float32), preferred_element_type=jnp.float32
    ).reshape(tokens, window, tile_up.shape[3])
    running = None
    for expert_number in range(window):
        gate_pre = jnp.dot(
            input_rows, gate_weight[expert_number], preferred_element_type=jnp.float32
        )
        up_value = (
            jnp.dot(input_rows, up_weight[expert_number], preferred_element_type=jnp.float32)
            + ADAPTER_SCALE * adapted_hidden[:, expert_number]
        )
        hidden = (weight[:, expert_number, None] * jax.nn.silu(gate_pre) * up_value).astype(
            jnp.bfloat16
        )
        gathered = lax.all_gather(hidden, "expert", axis=1, tiled=True)
        part = jnp.dot(gathered, down_weight[expert_number], preferred_element_type=jnp.float32)
        running = part if running is None else running + part
    mixed_rows = lax.psum_scatter(running, WIDE, scatter_dimension=0, tiled=True)
    return mixed_rows.astype(jnp.bfloat16)


def solution(mesh):
    groups = mesh.shape["groups"]
    wide = mesh.shape["wide"]
    expert = mesh.shape["expert"]
    split = Mesh(
        np.asarray(mesh.devices).reshape(groups, wide // 2, 2, expert),
        ("groups", "wy", "wc", "expert"),
    )
    rows = ("groups", "wy", "wc")
    in_specs = (
        P(rows, None, "expert"),
        P("groups"),
        P("groups", None),
        P("groups"),
        P("groups"),
        P(),
        P(None, None, GROUP),
        P(None, None, GROUP),
        P(None, WIDE, "expert"),
        P(rows, None, "expert", None),
        P("groups", None, None, GROUP),
    )
    out_specs = P(rows, "expert")
    return jax.shard_map(
        per_device, mesh=split, in_specs=in_specs, out_specs=out_specs, check_vma=False
    )
```

profile of v0, /device:TPU:0, one launch (start us, length us, event | category | flops | bytes accessed | tf_op | source)
XLA Modules:
  0.0 382.7 jit_solution(16340851096399354820)
XLA Ops:
  6.5 0.0 copy-start
  6.5 0.7 all-gather.5.cloned.1.call-update
  7.3 0.0 all-gather.7.cloned.1.call-start
  7.3 0.7 compare_and_fusion.2
  8.0 0.1 broadcast_bitcast_fusion
  8.1 0.1 dynamic-slice
  8.1 23.2 %all-gather.5.cloned.1.call-done = bf16[4,128,1536]{2,1,0:T(8,128)(2,1)} async-done(((bf16[1,128,1536]{2,1,0:T(8,128)(2,1)}), bf16[4,128,1536]{2,1,0:T(8,128)(2,1)}) %all-gather.5.cloned.1.call-update) | async-done | bytes 1572880 | tf_op jit(solution)/shard_map/all_gather | solution.py:34
  31.3 2.0 gather_fusion
  33.4 1.1 dynamic-slice_select_fusion
  34.5 0.0 all-gather.7.cloned.1.call-update
  34.5 0.0 all-reduce.2.cloned.1.call-start
  34.6 50.6 %all-gather.7.cloned.1.call-done = bf16[192,6144]{1,0:T(8,128)(2,1)} async-done(((bf16[192,1536]{1,0:T(8,128)(2,1)}), bf16[192,6144]{1,0:T(8,128)(2,1)}) %all-gather.7.cloned.1.call-update) | async-done | bytes 2359312 | tf_op jit(solution)/shard_map/all_gather | solution.py:38
  85.1 0.0 collective-permute-start
  85.1 0.0 copy-done.13
  85.2 0.6 gather_fusion.2
  85.9 0.0 copy-done.5
  85.9 1.8 gather_fusion.3
  87.7 0.2 broadcast_select_fusion.2
  87.8 0.0 copy-start.12
  87.8 1.1 copy-done.6
  88.9 0.5 fusion.33
  89.5 0.8 broadcast_select_fusion.3
  90.2 0.0 all-reduce.2.cloned.1.call-update
  90.2 0.0 all-gather.11.cloned.1.call-start
  90.3 0.6 gather_fusion.1
  90.9 88.2 %all-reduce.2.cloned.1.call-done = f32[3,128,2,64]{1,3,2,0:T(8,128)} async-done(((f32[3,128,2,64]{1,3,2,0:T(8,128)}), f32[3,128,2,64]{1,3,2,0:T(8,128)}) %all-reduce.2.cloned.1.call-update) | async-done | bytes 196624 | tf_op jit(solution)/shard_map/psum | solution.py:68
  179.1 1.6 convolution_bitcast_fusion
  180.7 0.4 copy.17
  181.1 0.0 copy-start.14
  181.1 0.0 collective-permute-done
  181.1 1.9 copy-done.7
  183.0 2.0 broadcast_select_fusion.1
  185.0 1.3 fusion.48
  186.4 8.1 %fusion.4 = f32[384,1024]{1,0:T(8,128)S(1)} fusion(bf16[2,6144,1024]{2,1,0:T(8,128)(2,1)} %param.17, bf16[192,6144]{1,0:T(8,128)(2,1)S(1)} %get-tuple-element.16, bf16[192,6144]{1,0:T(8,128)(2,1)S(1)} %get-tuple-element.15), kind=kOutput, calls=%fused_computation.8 | convolution fusion | flops 4841275392 | bytes 18874368 | tf_op jit(solution)/shard_map/dot_general | solution.py:75
  194.6 10.7 %fusion.24 = bf16[384,1024]{1,0:T(8,128)(2,1)} fusion(f32[384,2,1024]{2,0,1:T(8,128)S(1)} %bitcast.66, f32[384,1024]{1,0:T(8,128)S(1)} %fusion.4, bf16[2,6144,1024]{2,1,0:T(8,128)(2,1)} %param.18, f32[384]{0:T(512)S(1)} %get-tuple-element.6, bf16[192,6144]{1,0:T(8,128)(2,1)S(1)} %get-tuple-element.16, bf16[192,6144]{1,0:T(8,128)(2,1)S(1)} %get-tuple-element.15), kind=kOutput, calls=%fused_computation.31 | convolution fusion | flops 4844814336 | bytes 21235200 | tf_op jit(solution)/shard_map/dot_general | solution.py:79
  205.3 0.0 all-gather.11.cloned.1.call-update
  205.4 0.2 all-gather.9.cloned.1.call-start
  205.6 9.5 %fusion.10 = f32[384,1024]{1,0:T(8,128)S(1)} fusion(bf16[2,6144,1024]{2,1,0:T(8,128)(2,1)} %param.17, bf16[192,6144]{1,0:T(8,128)(2,1)} %copy-done.10, bf16[192,6144]{1,0:T(8,128)(2,1)} %copy-done.8), kind=kOutput, calls=%fused_computation.14 | convolution fusion | flops 4841275392 | bytes 18874368 | tf_op jit(solution)/shard_map/dot_general | solution.py:75
  215.2 10.8 %fusion.28 = bf16[384,1024]{1,0:T(8,128)(2,1)} fusion(f32[384,2,1024]{2,0,1:T(8,128)S(1)} %bitcast.67, f32[384,1024]{1,0:T(8,128)S(1)} %fusion.10, bf16[2,6144,1024]{2,1,0:T(8,128)(2,1)} %param.18, f32[384]{0:T(512)S(1)} %get-tuple-element.5, bf16[192,6144]{1,0:T(8,128)(2,1)S(1)} %copy-done.11, bf16[192,6144]{1,0:T(8,128)(2,1)S(1)} %copy-done.9), kind=kOutput, calls=%fused_computation.36 | convolution fusion | flops 4844814336 | bytes 21235200 | tf_op jit(solution)/shard_map/dot_general | solution.py:79
  226.0 0.0 all-gather.9.cloned.1.call-update
  226.0 0.0 reduce-scatter.2.cloned.1.call-start
  226.1 41.9 %all-gather.11.cloned.1.call-done = bf16[384,4096]{1,0:T(8,128)(2,1)} async-done(((bf16[384,1024]{1,0:T(8,128)(2,1)}), bf16[384,4096]{1,0:T(8,128)(2,1)}) %all-gather.11.cloned.1.call-update) | async-done | bytes 3145744 | tf_op jit(solution)/shard_map/all_gather | solution.py:85
  268.0 10.0 %fusion = f32[384,1536]{1,0:T(8,128)} fusion(bf16[384,4096]{1,0:T(8,128)(2,1)} %all-gather.11.cloned.1.call-done, bf16[2,4096,1536]{2,1,0:T(8,128)(2,1)} %param.19), kind=kOutput, calls=%fused_computation.4 | convolution fusion | flops 4831838208 | bytes 18087936 | tf_op jit(solution)/shard_map/dot_general | solution.py:86
  278.0 53.6 %all-gather.9.cloned.1.call-done = bf16[384,4096]{1,0:T(8,128)(2,1)} async-done(((bf16[384,1024]{1,0:T(8,128)(2,1)}), bf16[384,4096]{1,0:T(8,128)(2,1)}) %all-gather.9.cloned.1.call-update) | async-done | bytes 3145744 | tf_op jit(solution)/shard_map/all_gather | solution.py:85
  331.6 10.5 %fusion.18 = f32[384,1536]{1,0:T(8,128)} fusion(f32[384,1536]{1,0:T(8,128)} %fusion, bf16[384,4096]{1,0:T(8,128)(2,1)} %all-gather.9.cloned.1.call-done, bf16[2,4096,1536]{2,1,0:T(8,128)(2,1)} %param.19), kind=kOutput, calls=%fused_computation.23 | convolution fusion | flops 4832428032 | bytes 20447232 | tf_op jit(solution)/shard_map/dot_general | solution.py:86
  342.1 0.0 reduce-scatter.2.cloned.1.call-update
  342.1 31.9 %reduce-scatter.2.cloned.1.call-done = f32[96,1536]{1,0:T(8,128)} async-done(((f32[384,1536]{1,0:T(8,128)}), f32[96,1536]{1,0:T(8,128)}) %reduce-scatter.2.cloned.1.call-update) | async-done | bytes 589840 | tf_op jit(solution)/shard_map/reduce_scatter | solution.py:88
  374.0 1.8 convert_element_type.16
  (35 shorter events, 0.2 us)
Async XLA Ops:
  6.5 83.8 %copy-start = (bf16[8,2,64,1024]{3,2,1,0:T(8,128)(2,1)S(1)}, bf16[8,2,64,1024]{3,2,1,0:T(8,128)(2,1)}, u32[]{:S(2)}) copy-start(bf16[8,2,64,1024]{3,2,1,0:T(8,128)(2,1)} %param.21) | copy-start | bytes 6291460
  6.5 78.6 %copy-start.13 = (s32[3]{0:T(128)S(1)}, s32[3]{0:T(128)}, u32[]{:S(2)}) copy-start(s32[3]{0:T(128)} %param.14) | copy-start | bytes 40
  6.5 78.6 %copy-start.2 = (s32[8]{0:T(128)S(1)}, s32[8]{0:T(128)}, u32[]{:S(2)}) copy-start(s32[8]{0:T(128)} %param.15) | copy-start | bytes 100
  6.5 24.8 %all-gather.5.cloned.1.call-start = ((), (), s32[]{:S(2)}) async-start(), calls=%async_computation.1 | async-start | bytes 1966080 | tf_op jit(solution)/shard_map/all_gather | solution.py:34
  7.3 77.9 %all-gather.7.cloned.1.call-start = ((), (), s32[]{:S(2)}) async-start(), calls=%async_computation.2 | async-start | bytes 2949120 | tf_op jit(solution)/shard_map/all_gather | solution.py:38
  33.4 52.5 %copy-start.5 = (bf16[3,128,1536]{2,1,0:T(8,128)(2,1)}, bf16[3,128,1536]{2,1,0:T(8,128)(2,1)S(1)}, u32[]{:S(2)}) copy-start(bf16[3,128,1536]{2,1,0:T(8,128)(2,1)S(1)} %gather_fusion) | copy-start | bytes 3538948
  34.5 144.6 %all-reduce.2.cloned.1.call-start = ((), (), s32[]{:S(2)}) async-start(), calls=%async_computation.3 | async-start | bytes 393216 | tf_op jit(solution)/shard_map/psum | solution.py:68
  85.1 96.0 %collective-permute-start = (bf16[192,6144]{1,0:T(8,128)(2,1)}, bf16[192,6144]{1,0:T(8,128)(2,1)}, u32[]{:S(2)}, u32[]{:S(2)}) collective-permute-start(bf16[192,6144]{1,0:T(8,128)(2,1)} %all-gather.7.cloned.1.call-done), channel_id=1, source_target_pairs={{0,4},{4,0},{1,5},{5,1},{2,6},{6,2},{3,7},{7,3},{8,12},{12,8},{9,1... | collective-permute-start | bytes 7077896 | tf_op jit(solution)/shard_map/ppermute | solution.py:39
  87.6 1.3 copy-start.6
  87.8 2.5 copy-start.12
  90.2 177.7 %all-gather.11.cloned.1.call-start = ((), (), s32[]{:S(2)}) async-start(), calls=%async_computation.5 | async-start | bytes 3932160 | tf_op jit(solution)/shard_map/all_gather | solution.py:85
  180.7 2.3 copy-start.7
  181.1 13.5 %copy-start.3 = (f32[3,128,2,1024]{3,1,0,2:T(8,128)}, f32[3,128,2,1024]{3,1,0,2:T(8,128)S(1)}, u32[]{:S(2)}) copy-start(f32[3,128,2,1024]{3,1,0,2:T(8,128)S(1)} %copy.17) | copy-start | bytes 9437188
  181.1 3.9 %copy-start.14 = (bf16[6144,8]{0,1:T(8,128)(2,1)S(1)}, bf16[6144,8]{0,1:T(8,128)(2,1)}, u32[]{:S(2)}) copy-start(bf16[6144,8]{0,1:T(8,128)(2,1)} %param.16) | copy-start | bytes 294916
  185.0 9.6 %copy-start.8 = (bf16[192,6144]{1,0:T(8,128)(2,1)}, bf16[192,6144]{1,0:T(8,128)(2,1)S(1)}, u32[]{:S(2)}) copy-start(bf16[192,6144]{1,0:T(8,128)(2,1)S(1)} %get-tuple-element.15) | copy-start | bytes 7077892
  185.0 9.6 %copy-start.10 = (bf16[192,6144]{1,0:T(8,128)(2,1)}, bf16[192,6144]{1,0:T(8,128)(2,1)S(1)}, u32[]{:S(2)}) copy-start(bf16[192,6144]{1,0:T(8,128)(2,1)S(1)} %get-tuple-element.16) | copy-start | bytes 7077892
  205.4 126.2 %all-gather.9.cloned.1.call-start = ((), (), s32[]{:S(2)}) async-start(), calls=%async_computation.4 | async-start | bytes 3932160 | tf_op jit(solution)/shard_map/all_gather | solution.py:85
  205.6 9.6 %copy-start.4 = (f32[3,128,2,1024]{3,1,0,2:T(8,128)S(1)}, f32[3,128,2,1024]{3,1,0,2:T(8,128)}, u32[]{:S(2)}) copy-start(f32[3,128,2,1024]{3,1,0,2:T(8,128)} %copy-done.3) | copy-start | bytes 9437188
  205.6 9.6 %copy-start.9 = (bf16[192,6144]{1,0:T(8,128)(2,1)S(1)}, bf16[192,6144]{1,0:T(8,128)(2,1)}, u32[]{:S(2)}) copy-start(bf16[192,6144]{1,0:T(8,128)(2,1)} %copy-done.8) | copy-start | bytes 7077892
  205.6 9.6 %copy-start.11 = (bf16[192,6144]{1,0:T(8,128)(2,1)S(1)}, bf16[192,6144]{1,0:T(8,128)(2,1)}, u32[]{:S(2)}) copy-start(bf16[192,6144]{1,0:T(8,128)(2,1)} %copy-done.10) | copy-start | bytes 7077892
  226.0 148.0 %reduce-scatter.2.cloned.1.call-start = ((), (), s32[]{:S(2)}) async-start(), calls=%async_computation.6 | async-start | bytes 2949120 | tf_op jit(solution)/shard_map/reduce_scatter | solution.py:88
  331.6 44.3 %copy-start.1 = (bf16[8,2,64,1024]{3,2,1,0:T(8,128)(2,1)S(1)}, bf16[8,2,64,1024]{3,2,1,0:T(8,128)(2,1)}, u32[]{:S(2)}) copy-start(bf16[8,2,64,1024]{3,2,1,0:T(8,128)(2,1)} %param.21) | copy-start | bytes 6291460
Sparse Core Ops, SparseCore 0:
  8.9 22.3 all-gather.4
  34.6 50.4 all-gather.6
  90.4 88.7 all-reduce.1
  205.5 62.4 all-gather.10
  269.4 62.1 all-gather.8
  342.2 31.7 reduce-scatter.1
where the time goes:
time: 383 us
  waiting for transfers between devices  290 us (76%)
  matrix products  63.1 us (16%)
  between operations  13.8 us (4%)
  local copies, waits for them, and re-layouts  8.6 us (2%)
  other arithmetic  6.66 us (2%)
    all_gather x2, waiting for transfers between devices, per_device(): gathered = lax.all_gather(hidden, 'expert', axis=1, tiled=True)  95.5 us
    psum x1, waiting for transfers between devices, per_device(): lax.psum(partial_rank, GROUP)  88.2 us
    all_gather x1, waiting for transfers between devices, per_device(): mine = lax.all_gather(mine_q, 'expert', axis=1, tiled=True)  50.6 us
    reduce_scatter x1, waiting for transfers between devices, per_device(): lax.psum_scatter(running, WIDE, scatter_dimension=0, tiled=True)  31.9 us
    all_gather x1, waiting for transfers between devices, per_device(): slots_q = lax.all_gather(prompts, WIDE, axis=0, tiled=True)  23.2 us
    dot_general x2, matrix products, per_device(): jnp.dot(input_rows, up_weight[expert_number], preferred_element_type=jnp....  21.6 us
    dot_general x2, matrix products, per_device(): jnp.dot(gathered, down_weight[expert_number], preferred_element_type=jnp....  20.5 us
    dot_general x2, matrix products, per_device(): jnp.dot(input_rows, gate_weight[expert_number], preferred_element_type=jn...  17.7 us
  transfers between devices with their start and end apart: 7, of which 6 were waited for; matrix products, arithmetic and copies ran while one was open for 10% of the time, Pallas kernels for 0%

commit v1 on v0

--- a/solution.py
+++ b/solution.py
@@ -65,7 +65,9 @@
     partial_rank = jnp.where(
         (owners == wide_index)[:, None, None, None], partial_rank, jnp.zeros_like(partial_rank)
     )
-    lowrank = lax.reduce_precision(lax.psum(partial_rank, GROUP), exponent_bits=8, mantissa_bits=7)
+    lowrank = lax.reduce_precision(
+        jnp.sum(lax.all_gather(partial_rank, GROUP), axis=0), exponent_bits=8, mantissa_bits=7
+    )
     tile_up = jnp.take(adapter_up_weight, tile_tenant_index, axis=0)
     adapted_hidden = jnp.einsum(
         "nter,nerf->ntef", lowrank, tile_up.astype(jnp.float32), preferred_element_type=jnp.float32

time: 383 us -> 337 us (0.88)
  waiting for transfers between devices: 290 us -> 242 us
    psum x1 -> x0, waiting for transfers between devices: 88.2 us -> none  [per_device(): lax.psum(partial_rank, GROUP)]
    all_gather x0 -> x1, waiting for transfers between devices: none -> 45.7 us  [per_device(): lax.all_gather(partial_rank, GROUP)]
    all_gather x1, waiting for transfers between devices: 50.6 us -> 45.4 us  [per_device(): mine = lax.all_gather(mine_q, 'expert', axis=1, tiled=True)]
  transfers between devices with their start and end apart: 7 -> 7, of which waited for: 6 -> 6; matrix products, arithmetic and copies ran while one was open for 10% -> 12% of each run, Pallas kernels for 0% -> 0%
where the time goes in v1:
time: 337 us; the launch traced here: 336 us
  waiting for transfers between devices  242 us (72%)
  matrix products  62.2 us (18%)
  between operations  13.8 us (4%)
  other arithmetic  8.78 us (3%)
  local copies, waits for them, and re-layouts  8.61 us (3%)
    all_gather x2, waiting for transfers between devices, per_device(): gathered = lax.all_gather(hidden, 'expert', axis=1, tiled=True)  95.3 us
    all_gather x1, waiting for transfers between devices, per_device(): lax.all_gather(partial_rank, GROUP)  45.7 us
    all_gather x1, waiting for transfers between devices, per_device(): mine = lax.all_gather(mine_q, 'expert', axis=1, tiled=True)  45.4 us
    reduce_scatter x1, waiting for transfers between devices, per_device(): lax.psum_scatter(running, WIDE, scatter_dimension=0, tiled=True)  31.9 us
    all_gather x1, waiting for transfers between devices, per_device(): slots_q = lax.all_gather(prompts, WIDE, axis=0, tiled=True)  23.2 us
    dot_general x2, matrix products, per_device(): jnp.dot(input_rows, up_weight[expert_number], preferred_element_type=jnp....  21.6 us
    dot_general x2, matrix products, per_device(): jnp.dot(gathered, down_weight[expert_number], preferred_element_type=jnp....  20.5 us
    dot_general x2, matrix products, per_device(): jnp.dot(input_rows, gate_weight[expert_number], preferred_element_type=jn...  17.7 us
  transfers between devices with their start and end apart: 7, of which 6 were waited for; matrix products, arithmetic and copies ran while one was open for 12% of the time, Pallas kernels for 0%

profile of v1, /device:TPU:0, one launch (start us, length us, event | category | flops | bytes accessed | tf_op | source)
XLA Modules:
  0.0 336.1 jit_solution(3860571992430907327)
XLA Ops:
  6.5 0.7 all-gather.7.cloned.1.call-update
  7.3 0.0 all-gather.9.cloned.1.call-start
  7.3 0.7 compare_and_fusion.2
  8.0 0.1 broadcast_bitcast_fusion
  8.1 0.1 dynamic-slice
  8.1 23.2 %all-gather.7.cloned.1.call-done = bf16[4,128,1536]{2,1,0:T(8,128)(2,1)} async-done(((bf16[1,128,1536]{2,1,0:T(8,128)(2,1)}), bf16[4,128,1536]{2,1,0:T(8,128)(2,1)}) %all-gather.7.cloned.1.call-update) | async-done | bytes 1572880 | tf_op jit(solution)/shard_map/all_gather | solution.py:34
  31.3 2.0 gather_fusion
  33.4 1.2 dynamic-slice_select_fusion
  34.5 0.0 all-gather.9.cloned.1.call-update
  34.6 0.0 all-gather.15.cloned.1.call-start
  34.7 0.6 gather_fusion.2
  35.3 0.0 copy-done.5
  35.4 1.8 gather_fusion.3
  37.1 0.2 broadcast_select_fusion.2
  37.3 1.1 copy-done.6
  38.4 0.5 fusion.33
  38.9 0.8 broadcast_select_fusion.3
  39.7 0.0 all-gather.15.cloned.1.call-update
  39.7 0.0 all-gather.13.cloned.1.call-start
  39.8 45.4 %all-gather.9.cloned.1.call-done = bf16[192,6144]{1,0:T(8,128)(2,1)} async-done(((bf16[192,1536]{1,0:T(8,128)(2,1)}), bf16[192,6144]{1,0:T(8,128)(2,1)}) %all-gather.9.cloned.1.call-update) | async-done | bytes 2359312 | tf_op jit(solution)/shard_map/all_gather | solution.py:38
  85.2 0.0 collective-permute-start
  85.2 0.0 copy-done
  85.2 0.6 gather_fusion.1
  85.8 45.7 %all-gather.15.cloned.1.call-done = f32[48,128,2,64]{1,3,2,0:T(8,128)} async-done(((f32[3,128,2,64]{1,3,2,0:T(8,128)}), f32[48,128,2,64]{1,3,2,0:T(8,128)}) %all-gather.15.cloned.1.call-update) | async-done | bytes 3145744 | tf_op jit(solution)/shard_map/all_gather | solution.py:69
  131.5 2.1 reduce_sum.19
  133.6 0.6 convolution_bitcast_fusion
  134.3 0.0 copy-start.7
  134.3 0.4 copy.17
  134.7 0.0 copy-start.14
  134.7 0.0 collective-permute-done
  134.7 1.9 copy-done.7
  136.6 2.0 broadcast_select_fusion.1
  138.6 1.3 fusion.48
  140.0 8.1 %fusion.4 = f32[384,1024]{1,0:T(8,128)S(1)} fusion(bf16[2,6144,1024]{2,1,0:T(8,128)(2,1)} %param.17, bf16[192,6144]{1,0:T(8,128)(2,1)S(1)} %get-tuple-element.16, bf16[192,6144]{1,0:T(8,128)(2,1)S(1)} %get-tuple-element.15), kind=kOutput, calls=%fused_computation.8 | convolution fusion | flops 4841275392 | bytes 18874368 | tf_op jit(solution)/shard_map/dot_general | solution.py:77
  148.2 10.7 %fusion.24 = bf16[384,1024]{1,0:T(8,128)(2,1)} fusion(f32[384,2,1024]{2,0,1:T(8,128)S(1)} %bitcast.67, f32[384,1024]{1,0:T(8,128)S(1)} %fusion.4, bf16[2,6144,1024]{2,1,0:T(8,128)(2,1)} %param.18, f32[384]{0:T(512)S(1)} %get-tuple-element.6, bf16[192,6144]{1,0:T(8,128)(2,1)S(1)} %get-tuple-element.16, bf16[192,6144]{1,0:T(8,128)(2,1)S(1)} %get-tuple-element.15), kind=kOutput, calls=%fused_computation.31 | convolution fusion | flops 4844814336 | bytes 21235200 | tf_op jit(solution)/shard_map/dot_general | solution.py:81
  158.9 0.0 all-gather.13.cloned.1.call-update
  158.9 0.2 all-gather.11.cloned.1.call-start
  159.2 9.5 %fusion.10 = f32[384,1024]{1,0:T(8,128)S(1)} fusion(bf16[2,6144,1024]{2,1,0:T(8,128)(2,1)} %param.17, bf16[192,6144]{1,0:T(8,128)(2,1)} %copy-done.10, bf16[192,6144]{1,0:T(8,128)(2,1)} %copy-done.8), kind=kOutput, calls=%fused_computation.14 | convolution fusion | flops 4841275392 | bytes 18874368 | tf_op jit(solution)/shard_map/dot_general | solution.py:77
  168.8 10.8 %fusion.28 = bf16[384,1024]{1,0:T(8,128)(2,1)} fusion(f32[384,2,1024]{2,0,1:T(8,128)S(1)} %bitcast.68, f32[384,1024]{1,0:T(8,128)S(1)} %fusion.10, bf16[2,6144,1024]{2,1,0:T(8,128)(2,1)} %param.18, f32[384]{0:T(512)S(1)} %get-tuple-element.5, bf16[192,6144]{1,0:T(8,128)(2,1)S(1)} %copy-done.11, bf16[192,6144]{1,0:T(8,128)(2,1)S(1)} %copy-done.9), kind=kOutput, calls=%fused_computation.36 | convolution fusion | flops 4844814336 | bytes 21235200 | tf_op jit(solution)/shard_map/dot_general | solution.py:81
  179.6 0.0 all-gather.11.cloned.1.call-update
  179.6 0.0 reduce-scatter.2.cloned.1.call-start
  179.7 41.7 %all-gather.13.cloned.1.call-done = bf16[384,4096]{1,0:T(8,128)(2,1)} async-done(((bf16[384,1024]{1,0:T(8,128)(2,1)}), bf16[384,4096]{1,0:T(8,128)(2,1)}) %all-gather.13.cloned.1.call-update) | async-done | bytes 3145744 | tf_op jit(solution)/shard_map/all_gather | solution.py:87
  221.4 10.0 %fusion = f32[384,1536]{1,0:T(8,128)} fusion(bf16[384,4096]{1,0:T(8,128)(2,1)} %all-gather.13.cloned.1.call-done, bf16[2,4096,1536]{2,1,0:T(8,128)(2,1)} %param.19), kind=kOutput, calls=%fused_computation.4 | convolution fusion | flops 4831838208 | bytes 18087936 | tf_op jit(solution)/shard_map/dot_general | solution.py:88
  231.4 53.6 %all-gather.11.cloned.1.call-done = bf16[384,4096]{1,0:T(8,128)(2,1)} async-done(((bf16[384,1024]{1,0:T(8,128)(2,1)}), bf16[384,4096]{1,0:T(8,128)(2,1)}) %all-gather.11.cloned.1.call-update) | async-done | bytes 3145744 | tf_op jit(solution)/shard_map/all_gather | solution.py:87
  285.0 10.5 %fusion.18 = f32[384,1536]{1,0:T(8,128)} fusion(f32[384,1536]{1,0:T(8,128)} %fusion, bf16[384,4096]{1,0:T(8,128)(2,1)} %all-gather.11.cloned.1.call-done, bf16[2,4096,1536]{2,1,0:T(8,128)(2,1)} %param.19), kind=kOutput, calls=%fused_computation.23 | convolution fusion | flops 4832428032 | bytes 20447232 | tf_op jit(solution)/shard_map/dot_general | solution.py:88
  295.5 0.0 reduce-scatter.2.cloned.1.call-update
  295.5 31.9 %reduce-scatter.2.cloned.1.call-done = f32[96,1536]{1,0:T(8,128)} async-done(((f32[384,1536]{1,0:T(8,128)}), f32[96,1536]{1,0:T(8,128)}) %reduce-scatter.2.cloned.1.call-update) | async-done | bytes 589840 | tf_op jit(solution)/shard_map/reduce_scatter | solution.py:90
  327.4 1.8 convert_element_type.16
  (36 shorter events, 0.2 us)
Async XLA Ops:
  6.5 78.6 %copy-start = (bf16[8,2,64,1024]{3,2,1,0:T(8,128)(2,1)S(1)}, bf16[8,2,64,1024]{3,2,1,0:T(8,128)(2,1)}, u32[]{:S(2)}) copy-start(bf16[8,2,64,1024]{3,2,1,0:T(8,128)(2,1)} %param.21) | copy-start | bytes 6291460
  6.5 28.1 %copy-start.13 = (s32[3]{0:T(128)S(1)}, s32[3]{0:T(128)}, u32[]{:S(2)}) copy-start(s32[3]{0:T(128)} %param.14) | copy-start | bytes 40
  6.5 28.1 %copy-start.2 = (s32[8]{0:T(128)S(1)}, s32[8]{0:T(128)}, u32[]{:S(2)}) copy-start(s32[8]{0:T(128)} %param.15) | copy-start | bytes 100
  6.5 24.8 %all-gather.7.cloned.1.call-start = ((), (), s32[]{:S(2)}) async-start(), calls=%async_computation.1 | async-start | bytes 1966080 | tf_op jit(solution)/shard_map/all_gather | solution.py:34
  7.3 77.9 %all-gather.9.cloned.1.call-start = ((), (), s32[]{:S(2)}) async-start(), calls=%async_computation.2 | async-start | bytes 2949120 | tf_op jit(solution)/shard_map/all_gather | solution.py:38
  33.4 2.0 copy-start.5
  34.6 97.0 %all-gather.15.cloned.1.call-start = ((), (), s32[]{:S(2)}) async-start(), calls=%async_computation.6 | async-start | bytes 3342336 | tf_op jit(solution)/shard_map/all_gather | solution.py:69
  37.1 1.3 copy-start.6
  38.4 47.4 %copy-start.12 = (s32[384,2]{0,1:T(2,128)S(1)}, s32[384,2]{0,1:T(2,128)}, u32[]{:S(2)}) copy-start(s32[384,2]{0,1:T(2,128)} %param.13) | copy-start | bytes 9220
  39.7 181.6 %all-gather.13.cloned.1.call-start = ((), (), s32[]{:S(2)}) async-start(), calls=%async_computation.4 | async-start | bytes 3932160 | tf_op jit(solution)/shard_map/all_gather | solution.py:87
  85.2 49.5 %collective-permute-start = (bf16[192,6144]{1,0:T(8,128)(2,1)}, bf16[192,6144]{1,0:T(8,128)(2,1)}, u32[]{:S(2)}, u32[]{:S(2)}) collective-permute-start(bf16[192,6144]{1,0:T(8,128)(2,1)} %all-gather.9.cloned.1.call-done), channel_id=1, source_target_pairs={{0,4},{4,0},{1,5},{5,1},{2,6},{6,2},{3,7},{7,3},{8,12},{12,8},{9,1... | collective-permute-start | bytes 7077896 | tf_op jit(solution)/shard_map/ppermute | solution.py:39
  134.3 2.3 copy-start.7
  134.7 13.5 %copy-start.3 = (f32[3,128,2,1024]{3,1,0,2:T(8,128)}, f32[3,128,2,1024]{3,1,0,2:T(8,128)S(1)}, u32[]{:S(2)}) copy-start(f32[3,128,2,1024]{3,1,0,2:T(8,128)S(1)} %copy.17) | copy-start | bytes 9437188
  134.7 3.9 %copy-start.14 = (bf16[6144,8]{0,1:T(8,128)(2,1)S(1)}, bf16[6144,8]{0,1:T(8,128)(2,1)}, u32[]{:S(2)}) copy-start(bf16[6144,8]{0,1:T(8,128)(2,1)} %param.16) | copy-start | bytes 294916
  138.6 9.6 %copy-start.8 = (bf16[192,6144]{1,0:T(8,128)(2,1)}, bf16[192,6144]{1,0:T(8,128)(2,1)S(1)}, u32[]{:S(2)}) copy-start(bf16[192,6144]{1,0:T(8,128)(2,1)S(1)} %get-tuple-element.15) | copy-start | bytes 7077892
  138.6 9.6 %copy-start.10 = (bf16[192,6144]{1,0:T(8,128)(2,1)}, bf16[192,6144]{1,0:T(8,128)(2,1)S(1)}, u32[]{:S(2)}) copy-start(bf16[192,6144]{1,0:T(8,128)(2,1)S(1)} %get-tuple-element.16) | copy-start | bytes 7077892
  158.9 126.0 %all-gather.11.cloned.1.call-start = ((), (), s32[]{:S(2)}) async-start(), calls=%async_computation.3 | async-start | bytes 3932160 | tf_op jit(solution)/shard_map/all_gather | solution.py:87
  159.2 9.6 %copy-start.4 = (f32[3,128,2,1024]{3,1,0,2:T(8,128)S(1)}, f32[3,128,2,1024]{3,1,0,2:T(8,128)}, u32[]{:S(2)}) copy-start(f32[3,128,2,1024]{3,1,0,2:T(8,128)} %copy-done.3) | copy-start | bytes 9437188
  159.2 9.6 %copy-start.9 = (bf16[192,6144]{1,0:T(8,128)(2,1)S(1)}, bf16[192,6144]{1,0:T(8,128)(2,1)}, u32[]{:S(2)}) copy-start(bf16[192,6144]{1,0:T(8,128)(2,1)} %copy-done.8) | copy-start | bytes 7077892
  159.2 9.6 %copy-start.11 = (bf16[192,6144]{1,0:T(8,128)(2,1)S(1)}, bf16[192,6144]{1,0:T(8,128)(2,1)}, u32[]{:S(2)}) copy-start(bf16[192,6144]{1,0:T(8,128)(2,1)} %copy-done.10) | copy-start | bytes 7077892
  179.6 147.8 %reduce-scatter.2.cloned.1.call-start = ((), (), s32[]{:S(2)}) async-start(), calls=%async_computation.5 | async-start | bytes 2949120 | tf_op jit(solution)/shard_map/reduce_scatter | solution.py:90
  285.0 44.2 %copy-start.1 = (bf16[8,2,64,1024]{3,2,1,0:T(8,128)(2,1)S(1)}, bf16[8,2,64,1024]{3,2,1,0:T(8,128)(2,1)}, u32[]{:S(2)}) copy-start(bf16[8,2,64,1024]{3,2,1,0:T(8,128)(2,1)} %param.21) | copy-start | bytes 6291460
Sparse Core Ops, SparseCore 0:
  8.9 22.3 all-gather.6
  34.7 50.4 all-gather.8
  87.5 44.0 all-gather.14
  159.1 62.2 all-gather.12
  222.8 62.1 all-gather.10
  295.6 31.7 reduce-scatter.1
